TPU v7x, 32 devices: a whole 2x2x4 slice. The times are simulated.
32 devices in a mesh: groups: 2 (over y), video: 4 (over z), tensor: 4 (over x, core).
Axes of the slice: x: 2, y: 2, z: 4, core: 2. Of those that a mesh axis runs over, the one named last changes fastest.
Arguments:
- frames: bfloat16 [24, 256, 6144], P(('groups', 'video')), parts along dimension 0, may hold values from -610 to 610
- frame_video: int32 [24], P(('groups', 'video')), parts along dimension 0, may hold values from 0 to 3, never falling along the last dimension, each value on 1 to 6 neighbouring positions
- qkv_weight: bfloat16 [6144, 3, 3072], P('video', None, 'tensor'), may hold values from -0.078125 to 0.078125
- conn_weight: bfloat16 [3072, 3, 4096], P('tensor', None, 'video'), may hold values from -6 to 6
Outputs:
- summary: bfloat16 [384, 4096], P(('groups', 'video'), 'tensor'), parts along dimension 0
There are 2 independent parts, one for each index of `groups`. A program takes and returns all parts, laid end to end along the dimension named above; an argument that names none is the same for every part. Nothing has to cross between parts.
All inputs are finite; a program needn't handle non-finite values.
Results may differ from a plain program's by a relative error of at most 0.009.
Values may be sent and summed in bfloat16 or wider, within the bound.
No kernel may reach another device: no remote copies, remote signals or barrier semaphores. Data moves between devices by JAX's collectives and lax.ppermute only.
A program may use at most 192 MiB of HBM per device.

v0:
```python
import math
import jax
import jax.numpy as jnp
from jax import lax
from jax.sharding import PartitionSpec as P

HD = 128
PATCH = 256
POOL = 16


def rms_norm(values):
    return values * lax.rsqrt(jnp.mean(values * values, axis=-1, keepdims=True) + 1e-06)


def per_device(frames, frame_video, qkv_weight, conn_weight):
    scale = 1.0 / math.sqrt(HD)
    blocks = math.isqrt(POOL)
    inner = math.isqrt(PATCH) // blocks
    nframes = frames.shape[0]
    patch_rows = nframes * PATCH
    wide = frames.astype(jnp.float32)
    center = wide - jnp.mean(wide, axis=-1, keepdims=True)
    normed = center * lax.rsqrt(jnp.mean(center * center, axis=-1, keepdims=True) + 1e-06)
    normed = normed.astype(jnp.bfloat16).reshape(patch_rows, frames.shape[2])
    local_cols = qkv_weight.shape[1] * qkv_weight.shape[2]
    piece = lax.all_gather(qkv_weight, "video", axis=0, tiled=True)
    proj = jnp.dot(
        normed, piece.reshape(piece.shape[0], local_cols), preferred_element_type=jnp.float32
    )
    heads_local = qkv_weight.shape[2] // HD
    proj = proj.reshape(nframes, PATCH, 3, heads_local, HD)
    query = rms_norm(proj[:, :, 0]).astype(jnp.bfloat16)
    keys = rms_norm(proj[:, :, 1]).astype(jnp.bfloat16)
    values = proj[:, :, 2].astype(jnp.bfloat16)
    scores = jnp.einsum("fphd,fkhd->fhpk", query, keys, preferred_element_type=jnp.float32) * scale
    probs = jnp.exp(scores)
    probs = (probs / jnp.sum(probs, axis=-1, keepdims=True)).astype(jnp.bfloat16)
    attended = jnp.einsum("fhpk,fkhd->fphd", probs, values, preferred_element_type=jnp.float32)
    grid = attended.reshape(nframes, blocks, inner, blocks, inner, heads_local, HD)
    pooled = (
        jnp.mean(grid, axis=(2, 4)).reshape(nframes * POOL, heads_local * HD).astype(jnp.bfloat16)
    )
    rows = nframes * POOL
    partial_proj = jnp.einsum(
        "rc,ckt->rkt",
        pooled,
        lax.all_gather(conn_weight, "video", axis=2, tiled=True),
        preferred_element_type=jnp.float32,
    )
    clip_proj = lax.psum_scatter(
        partial_proj.astype(jnp.bfloat16), "tensor", scatter_dimension=2, tiled=True
    ).astype(jnp.float32)
    t_heads = clip_proj.shape[2] // HD
    tquery = rms_norm(clip_proj[:, 0].reshape(rows, t_heads, HD)).astype(jnp.bfloat16)
    tkey = rms_norm(clip_proj[:, 1].reshape(rows, t_heads, HD)).astype(jnp.bfloat16)
    tvalue = clip_proj[:, 2].astype(jnp.bfloat16)
    tkey_flat = tkey.reshape(rows, t_heads * HD)
    seg_rows = jnp.repeat(frame_video, POOL)
    query_frame = lax.axis_index("video") * nframes + jnp.arange(rows, dtype=jnp.int32) // POOL
    key_part = lax.all_gather(tkey_flat, "video", axis=0, tiled=True)
    value_part = lax.all_gather(tvalue, "video", axis=0, tiled=True)
    seg_part = lax.all_gather(seg_rows, "video", axis=0, tiled=True)
    count = key_part.shape[0]
    key_frame = jnp.arange(count, dtype=jnp.int32) // POOL
    allowed = (seg_part[None, :] == seg_rows[:, None]) & (
        key_frame[None, :] <= query_frame[:, None]
    )
    logits = (
        jnp.einsum(
            "rhd,khd->hrk",
            tquery,
            key_part.reshape(count, t_heads, HD),
            preferred_element_type=jnp.float32,
        )
        * scale
    )
    weights = jnp.where(allowed[None], jnp.exp(logits), jnp.float32(0.0))
    numer = jnp.einsum(
        "hrk,khd->rhd",
        weights.astype(jnp.bfloat16),
        value_part.reshape(count, t_heads, HD),
        preferred_element_type=jnp.float32,
    )
    denom = jnp.sum(weights, axis=-1)
    numer, denom = (numer, denom)
    summary = numer / jnp.transpose(denom)[:, :, None]
    return summary.reshape(rows, t_heads * HD).astype(jnp.bfloat16)


def solution(mesh):
    return jax.shard_map(
        per_device,
        mesh=mesh,
        in_specs=(
            P(("groups", "video"), None, None),
            P(("groups", "video")),
            P("video", None, "tensor"),
            P("tensor", None, "video"),
        ),
        out_specs=P(("groups", "video"), "tensor"),
        check_vma=False,
    )
```

profile of v0, /device:TPU:0, one launch (start us, length us, event | category | flops | bytes accessed | tf_op | source)
XLA Modules:
  0.0 894.5 jit_solution(1376324522640257826)
XLA Ops:
  6.5 10.3 %copy.32 = bf16[1536,3,768]{0,2,1:T(8,128)(2,1)} copy(bf16[1536,3,768]{2,0,1:T(8,128)(2,1)} %param.6) | data formatting | bytes 14155776 | tf_op args[2]
  16.9 0.7 all-gather.6.cloned.1.call-update
  17.7 5.2 convert_reduce_fusion
  22.9 1.2 copy-done
  24.0 2.6 fusion.2
  26.6 469.2 %all-gather.4.cloned.1.call-done = bf16[6144,3,768]{0,2,1:T(8,128)(2,1)} async-done(((bf16[1536,3,768]{0,2,1:T(8,128)(2,1)}), bf16[6144,3,768]{0,2,1:T(8,128)(2,1)}) %all-gather.4.cloned.1.call-update) | async-done | bytes 28311568 | tf_op jit(solution)/shard_map/all_gather | solution.py:27
  495.8 29.8 %fusion.5 = f32[3,256,3,6,128]{1,4,3,2,0:T(8,128)S(1)} fusion(bf16[3,6,128,6144,1]{3,2,1,0,4:T(8,128)(2,1)} %bitcast.92, bf16[3,256,6144]{2,1,0:T(8,128)(2,1)} %param.4, f32[3,256]{1,0:T(4,128)S(1)} %add_rsqrt_fusion.4, f32[3,256]{1,0:T(4,128)S(1)} %broadcast_multiply_fusion), kind=kOutput, calls=%fused_computation.7 | convolution fusion | flops 21762146304 | bytes 44832768 | tf_op jit(solution)/shard_map/dot_general | solution.py:28
  525.7 0.5 multiply_reduce_fusion.1
  526.2 1.2 fusion.9
  527.4 2.4 fusion.11
  529.7 2.0 copy.36
  531.8 1.0 reduce_sum.86
  532.8 0.1 reshape.178
  533.0 285.3 %all-gather.6.cloned.1.call-done = bf16[768,3,4096]{2,0,1:T(8,128)(2,1)} async-done(((bf16[768,3,1024]{2,0,1:T(8,128)(2,1)}), bf16[768,3,4096]{2,0,1:T(8,128)(2,1)}) %all-gather.6.cloned.1.call-update) | async-done | bytes 18874384 | tf_op jit(solution)/shard_map/all_gather | solution.py:48
  818.2 10.8 %convolution_convert_fusion = bf16[48,3,4096]{2,0,1:T(8,128)(2,1)} fusion(bf16[48,768,1]{1,0,2:T(8,128)(2,1)S(1)} %reshape.178, bf16[768,3,4096]{2,0,1:T(8,128)(2,1)} %all-gather.6.cloned.1.call-done), kind=kOutput, calls=%fused_computation.10 | convolution fusion | flops 906559488 | bytes 20127744 | tf_op jit(solution)/shard_map/rc,ckt->rkt/dot_general | solution.py:45
  829.1 0.1 reshape.171
  829.2 0.6 dynamic-slice
  830.5 0.2 dynamic-update-slice
  830.7 7.2 all-reduce
  838.0 15.8 %reduce-scatter.2.cloned.1.call-done = bf16[48,3,1024]{2,0,1:T(8,128)(2,1)} async-done(((bf16[48,3,4096]{2,0,1:T(8,128)(2,1)}), bf16[48,3,1024]{2,0,1:T(8,128)(2,1)}) %reduce-scatter.2.cloned.1.call-update) | async-done | bytes 294928 | tf_op jit(solution)/shard_map/reduce_scatter | solution.py:51
  853.7 0.9 slice.31
  854.6 14.5 %all-gather = bf16[192,1,1024]{2,0,1:T(8,128)(2,1)S(1)} all-gather(bf16[48,1,1024]{2,0,1:T(8,128)(2,1)S(1)} %slice.31), channel_id=2, replica_groups=mesh['groups'=2,'video'=4,'tensor'=4] {'video'}, dimensions={0}, use_global_device_ids=true | all-gather | bytes 491520 | tf_op jit(solution)/shard_map/all_gather | solution.py:62
  869.2 1.0 convert_element_type.61
  870.3 0.1 multiply_reduce_fusion.2
  870.6 0.1 multiply_convert_fusion.4
  870.8 0.1 reduce_sum.88
  871.0 0.1 copy.41
  871.1 0.1 mul.101
  871.2 15.4 %all_gather.19 = bf16[192,1024]{1,0:T(8,128)(2,1)S(1)} all-gather(bf16[48,1024]{1,0:T(8,128)(2,1)S(1)} %fusion.25), channel_id=1, replica_groups=mesh['groups'=2,'video'=4,'tensor'=4] {'video'}, dimensions={0}, use_global_device_ids=true | all-gather | bytes 491520 | tf_op jit(solution)/shard_map/all_gather | solution.py:61
  886.6 0.5 fusion.30
  887.1 0.3 fusion.21
  887.3 0.7 copy.70
  (30 shorter events, 0.8 us)
Async XLA Ops:
  6.5 489.3 %all-gather.4.cloned.1.call-start = ((), (), s32[]{:S(2)}) async-start(), calls=%async_computation.1 | async-start | bytes 35389440 | tf_op jit(solution)/shard_map/all_gather | solution.py:27
  16.9 801.4 %all-gather.6.cloned.1.call-start = ((), (), s32[]{:S(2)}) async-start(), calls=%async_computation.2 | async-start | bytes 23592960 | tf_op jit(solution)/shard_map/all_gather | solution.py:48
  17.6 836.1 %reduce-scatter.2.cloned.1.call-start = ((), (), s32[]{:S(2)}) async-start(), calls=%async_computation.3 | async-start | bytes 1474560 | tf_op jit(solution)/shard_map/reduce_scatter | solution.py:51
  17.7 6.4 copy-start
  532.9 296.1 %copy-start.1 = (s32[3]{0:T(128)S(1)}, s32[3]{0:T(128)}, u32[]{:S(2)}) copy-start(s32[3]{0:T(128)} %param.5) | copy-start | bytes 40
  533.0 296.2 %copy-start.2 = (u32[32]{0:T(128)S(1)}, u32[32]{0:T(128)}, u32[]{:S(2)}) copy-start(u32[32]{0:T(128)} %constant.63) | copy-start | bytes 388
Sparse Core Ops, SparseCore 0:
  17.0 478.8 all-gather.3
  497.4 320.7 all-gather.5
  829.2 24.5 reduce-scatter.1
where the time goes:
time: 895 us
  waiting for transfers between devices  771 us (86%)
  matrix products  44.8 us (5%)
  blocking collectives  37.1 us (4%)
  local copies, waits for them, and re-layouts  16.8 us (2%)
  between operations  14 us (2%)
  other arithmetic  10.9 us (1%)
    all_gather x1, waiting for transfers between devices, per_device(): piece = lax.all_gather(qkv_weight, 'video', axis=0, tiled=True)  469 us
    all_gather x1, waiting for transfers between devices, per_device(): lax.all_gather(conn_weight, 'video', axis=2, tiled=True)  285 us
    dot_general x1, matrix products, per_device(): jnp.dot(normed, piece.reshape(piece.shape[0], local_cols), preferred_elem...  29.8 us
  transfers between devices with their start and end apart: 3, of which 3 were waited for; matrix products, arithmetic and copies ran while one was open for 5% of the time, Pallas kernels for 0%

commit v1 on v0

--- a/solution.py
+++ b/solution.py
@@ -58,8 +58,11 @@
     tkey_flat = tkey.reshape(rows, t_heads * HD)
     seg_rows = jnp.repeat(frame_video, POOL)
     query_frame = lax.axis_index("video") * nframes + jnp.arange(rows, dtype=jnp.int32) // POOL
-    key_part = lax.all_gather(tkey_flat, "video", axis=0, tiled=True)
-    value_part = lax.all_gather(tvalue, "video", axis=0, tiled=True)
+    key_part, value_part = jnp.split(
+        lax.all_gather(jnp.concatenate([tkey_flat, tvalue], axis=1), "video", axis=0, tiled=True),
+        [tkey_flat.shape[1]],
+        axis=1,
+    )
     seg_part = lax.all_gather(seg_rows, "video", axis=0, tiled=True)
     count = key_part.shape[0]
     key_frame = jnp.arange(count, dtype=jnp.int32) // POOL

time: 895 us -> 885 us (0.989)
  blocking collectives: 37.1 us -> 26.8 us
    all_gather x2 -> x1, blocking collectives: 29.9 us -> 19.6 us  [per_device(): lax.all_gather(jnp.concatenate([tkey_flat, tvalue], axis=1), 'video', axi...]
where the time goes in v1:
time: 885 us; the launch traced here: 884 us
  waiting for transfers between devices  771 us (87%)
  matrix products  44.8 us (5%)
  blocking collectives  26.8 us (3%)
  local copies, waits for them, and re-layouts  16.8 us (2%)
  between operations  14 us (2%)
  other arithmetic  10.9 us (1%)
    all_gather x1, waiting for transfers between devices, per_device(): piece = lax.all_gather(qkv_weight, 'video', axis=0, tiled=True)  469 us
    all_gather x1, waiting for transfers between devices, per_device(): lax.all_gather(conn_weight, 'video', axis=2, tiled=True)  285 us
    dot_general x1, matrix products, per_device(): jnp.dot(normed, piece.reshape(piece.shape[0], local_cols), preferred_elem...  29.8 us
    all_gather x1, blocking collectives, per_device(): lax.all_gather(jnp.concatenate([tkey_flat, tvalue], axis=1), 'video', axi...  19.6 us
  transfers between devices with their start and end apart: 3, of which 3 were waited for; matrix products, arithmetic and copies ran while one was open for 5% of the time, Pallas kernels for 0%

profile of v1, /device:TPU:0, one launch (start us, length us, event | category | flops | bytes accessed | tf_op | source)
XLA Modules:
  0.0 884.2 jit_solution(17778950524951157956)
XLA Ops:
  6.5 10.3 %copy.32 = bf16[1536,3,768]{0,2,1:T(8,128)(2,1)} copy(bf16[1536,3,768]{2,0,1:T(8,128)(2,1)} %param.6) | data formatting | bytes 14155776 | tf_op args[2]
  16.9 0.7 all-gather.5.cloned.1.call-update
  17.7 5.2 convert_reduce_fusion
  22.9 1.2 copy-done
  24.0 2.6 fusion.2
  26.6 469.2 %all-gather.3.cloned.1.call-done = bf16[6144,3,768]{0,2,1:T(8,128)(2,1)} async-done(((bf16[1536,3,768]{0,2,1:T(8,128)(2,1)}), bf16[6144,3,768]{0,2,1:T(8,128)(2,1)}) %all-gather.3.cloned.1.call-update) | async-done | bytes 28311568 | tf_op jit(solution)/shard_map/all_gather | solution.py:27
  495.8 29.8 %fusion.5 = f32[3,256,3,6,128]{1,4,3,2,0:T(8,128)S(1)} fusion(bf16[3,6,128,6144,1]{3,2,1,0,4:T(8,128)(2,1)} %bitcast.91, bf16[3,256,6144]{2,1,0:T(8,128)(2,1)} %param.4, f32[3,256]{1,0:T(4,128)S(1)} %add_rsqrt_fusion.4, f32[3,256]{1,0:T(4,128)S(1)} %broadcast_multiply_fusion), kind=kOutput, calls=%fused_computation.7 | convolution fusion | flops 21762146304 | bytes 44832768 | tf_op jit(solution)/shard_map/dot_general | solution.py:28
  525.7 0.5 multiply_reduce_fusion.1
  526.2 1.2 fusion.9
  527.4 2.4 fusion.11
  529.7 2.0 copy.36
  531.8 1.0 reduce_sum.86
  532.8 0.1 reshape.176
  533.0 285.3 %all-gather.5.cloned.1.call-done = bf16[768,3,4096]{2,0,1:T(8,128)(2,1)} async-done(((bf16[768,3,1024]{2,0,1:T(8,128)(2,1)}), bf16[768,3,4096]{2,0,1:T(8,128)(2,1)}) %all-gather.5.cloned.1.call-update) | async-done | bytes 18874384 | tf_op jit(solution)/shard_map/all_gather | solution.py:48
  818.2 10.8 %convolution_convert_fusion = bf16[48,3,4096]{2,0,1:T(8,128)(2,1)} fusion(bf16[48,768,1]{1,0,2:T(8,128)(2,1)S(1)} %reshape.176, bf16[768,3,4096]{2,0,1:T(8,128)(2,1)} %all-gather.5.cloned.1.call-done), kind=kOutput, calls=%fused_computation.10 | convolution fusion | flops 906559488 | bytes 20127744 | tf_op jit(solution)/shard_map/rc,ckt->rkt/dot_general | solution.py:45
  829.1 0.1 reshape.169
  829.2 0.6 dynamic-slice
  830.5 0.2 dynamic-update-slice
  830.7 7.2 all-reduce
  838.0 15.8 %reduce-scatter.2.cloned.1.call-done = bf16[48,3,1024]{2,0,1:T(8,128)(2,1)} async-done(((bf16[48,3,4096]{2,0,1:T(8,128)(2,1)}), bf16[48,3,1024]{2,0,1:T(8,128)(2,1)}) %reduce-scatter.2.cloned.1.call-update) | async-done | bytes 294928 | tf_op jit(solution)/shard_map/reduce_scatter | solution.py:51
  853.7 1.0 convert_element_type.60
  854.8 0.1 reduce_sum.87
  855.0 0.1 copy.39
  855.1 0.1 mul.97
  855.3 0.9 slice_bitcast_fusion.5
  856.2 19.6 %all_gather.14 = bf16[192,2048]{1,0:T(8,128)(2,1)S(1)} all-gather(bf16[48,2048]{1,0:T(8,128)(2,1)S(1)} %pad_maximum_fusion), channel_id=1, replica_groups=mesh['groups'=2,'video'=4,'tensor'=4] {'video'}, dimensions={0}, use_global_device_ids=true | all-gather | bytes 983040 | tf_op jit(solution)/shard_map/all_gather | solution.py:62
  875.9 0.1 multiply_reduce_fusion.2
  876.1 0.1 copy.41
  876.2 0.1 multiply_convert_fusion.4
  876.3 0.5 fusion.31
  876.8 0.3 fusion.21
  877.0 0.7 copy.72
  (30 shorter events, 0.7 us)
Async XLA Ops:
  6.5 489.3 %all-gather.3.cloned.1.call-start = ((), (), s32[]{:S(2)}) async-start(), calls=%async_computation.1 | async-start | bytes 35389440 | tf_op jit(solution)/shard_map/all_gather | solution.py:27
  16.9 801.4 %all-gather.5.cloned.1.call-start = ((), (), s32[]{:S(2)}) async-start(), calls=%async_computation.2 | async-start | bytes 23592960 | tf_op jit(solution)/shard_map/all_gather | solution.py:48
  17.6 836.1 %reduce-scatter.2.cloned.1.call-start = ((), (), s32[]{:S(2)}) async-start(), calls=%async_computation.3 | async-start | bytes 1474560 | tf_op jit(solution)/shard_map/reduce_scatter | solution.py:51
  17.7 6.4 copy-start
  532.9 296.1 %copy-start.1 = (s32[3]{0:T(128)S(1)}, s32[3]{0:T(128)}, u32[]{:S(2)}) copy-start(s32[3]{0:T(128)} %param.5) | copy-start | bytes 40
  533.0 296.2 %copy-start.2 = (u32[32]{0:T(128)S(1)}, u32[32]{0:T(128)}, u32[]{:S(2)}) copy-start(u32[32]{0:T(128)} %constant.63) | copy-start | bytes 388
Sparse Core Ops, SparseCore 0:
  17.0 478.8 all-gather.2
  497.4 320.7 all-gather.4
  829.2 24.5 reduce-scatter.1
